TPU v7x, 32 devices: a whole 2x2x4 slice. The times are simulated.
32 devices in a mesh: grid: 8 (over z, x), mem: 4 (over y, core).
Axes of the slice: x: 2, y: 2, z: 4, core: 2. Of those that a mesh axis runs over, the one named last changes fastest.
Arguments:
- members: bfloat16 [80, 4, 16, 512], P('mem', None, 'grid'), may hold values from -0.8984375 to 0.8984375
- innovation: float32 [4, 16, 512], P(None, 'grid'), may hold values from -6 to 6
- observed_count: int32 [16, 512], P('grid'), may hold values from 0 to 3
- obs_precision: float32 [4], replicated, may hold values from 0.5 to 4
Outputs:
- recentred: bfloat16 [80, 4, 16, 512], P('mem', None, 'grid')
- increment: float32 [4, 16, 512], P('mem', 'grid')
All inputs are finite; a program needn't handle non-finite values.
Results may differ from a plain program's by a relative error of at most 0.0004.
Values may be sent and summed in bfloat16 or wider, within the bound.
No kernel may reach another device: no remote copies, remote signals or barrier semaphores. Data moves between devices by JAX's collectives and lax.ppermute only.
A program may use at most 64 MiB of HBM per device.

v0:
```python
import jax
import jax.numpy as jnp
from jax import lax
from jax.sharding import PartitionSpec as P

PASSES = 2
ITERS = 2
diffusion = 0.25


def padded(value, sides, width):
    for axis, dim in sides:
        devices, length = (lax.axis_size(axis), value.shape[dim])
        up = [(i, (i + 1) % devices) for i in range(devices - 1)]
        down = [(j, i) for i, j in up]
        last = lax.slice_in_dim(value, length - width, length, axis=dim)
        leading = lax.slice_in_dim(value, 0, width, axis=dim)
        before = lax.ppermute(last, axis, up)
        after = lax.ppermute(leading, axis, down)
        value = jnp.concatenate([before, value, after], axis=dim)
    return value


def smooth(field):
    for sweep_index in range(PASSES):
        extended = padded(field, (("grid", 2),), 1)
        centre = extended[:, :, 1:-1]
        field = centre + diffusion * (extended[:, :, :-2] + extended[:, :, 2:] - 2.0 * centre)
    for sweep_index in range(PASSES):
        field = field + diffusion * (jnp.roll(field, 1, 3) + jnp.roll(field, -1, 3) - 2.0 * field)
    return field


def member_total(product):
    summed = jnp.sum(product, axis=0)
    return summed


def norm_of(residual):
    return lax.psum(jnp.sum(residual * residual), ("grid", "mem"))


def local(members, innovation, observed_count, obs_precision):
    mem_index = lax.axis_index("mem")
    level_share = members.shape[1] // lax.axis_size("mem")
    perturbed = lax.all_to_all(members, "mem", split_axis=1, concat_axis=0, tiled=True)
    precision = lax.dynamic_slice_in_dim(obs_precision, mem_index * level_share, level_share, 0)
    local_innovation = lax.dynamic_slice_in_dim(innovation, mem_index * level_share, level_share, 0)
    weight = observed_count.astype(jnp.float32)[None] * precision[:, None, None]
    gradient = smooth(perturbed * (weight * local_innovation)[None])
    carried = jnp.zeros_like(gradient)
    residual = gradient
    direction = residual
    norm_now = norm_of(residual)
    for iteration in range(ITERS):
        smoothed = smooth(direction)
        total = member_total(perturbed * smoothed)
        back = smooth(perturbed * (weight * total)[None])
        image, smoothed = (direction + back, smoothed)
        step_size = norm_now / lax.psum(jnp.sum(direction * image), ("grid", "mem"))
        carried = carried + step_size * smoothed
        residual = residual - step_size * image
        if iteration + 1 < ITERS:
            norm_next = norm_of(residual)
            direction = residual + norm_next / norm_now * direction
            norm_now = norm_next
    increment = member_total(perturbed * carried)
    whole = lax.all_gather(increment, "mem", axis=0, tiled=True)
    recentred = (members.astype(jnp.float32) + whole[None]).astype(jnp.bfloat16)
    return (recentred, increment)


def smooth_rows(field):
    for sweep_index in range(PASSES):
        edge = jnp.zeros_like(field[..., :1, :])
        north = jnp.concatenate([edge, field[..., :-1, :]], axis=-2)
        south = jnp.concatenate([field[..., 1:, :], edge], axis=-2)
        field = field + diffusion * (north + south - 2.0 * field)
    for sweep_index in range(PASSES):
        field = field + diffusion * (jnp.roll(field, 1, -1) + jnp.roll(field, -1, -1) - 2.0 * field)
    return field


def all_sum(values):
    devices = lax.axis_size("grid") * lax.axis_size("mem")
    row = jnp.zeros((128,), jnp.float32).at[: values.shape[0]].set(values)
    gathered = lax.all_to_all(
        jnp.broadcast_to(row, (devices, 128)), ("grid", "mem"), 0, 0, tiled=True
    )
    return jnp.sum(gathered, axis=0)


def local_by_level(members, innovation, observed_count, obs_precision):
    grid_size = lax.axis_size("grid")
    mem_size = lax.axis_size("mem")
    count, levels, rows, nlon = members.shape
    copies = grid_size // levels
    nlat = rows * grid_size
    grid_index = lax.axis_index("grid")
    mem_index = lax.axis_index("mem")
    level = grid_index // copies
    chunk_level = [j // copies for j in range(grid_size)]
    sent = jnp.stack([members[:, l] for l in chunk_level], axis=0)
    got = lax.all_to_all(sent, "grid", 0, 0, tiled=True)
    mine = jnp.transpose(got, (1, 0, 2, 3)).reshape(count, nlat, nlon)
    extra = jnp.stack(
        [jnp.stack([innovation[l], observed_count.astype(jnp.float32)]) for l in chunk_level],
        axis=0,
    )
    extra = lax.all_to_all(extra, "grid", 0, 0, tiled=True)
    extra = jnp.transpose(extra, (1, 0, 2, 3)).reshape(2, nlat, nlon)
    precision = lax.dynamic_index_in_dim(obs_precision, level, 0, keepdims=False)
    weight = extra[1] * precision
    widened = mine.astype(jnp.float32)
    span = nlat // copies
    own = lax.broadcasted_iota(jnp.int32, (nlat, nlon), 0) // span == grid_index % copies
    first = mem_index == 0

    def squares(field):
        return jnp.sum(jnp.where(own[None], field * field, 0.0))

    def weighted(total):
        return jnp.where(first, jnp.sum(jnp.where(own, weight * total * total, 0.0)), 0.0)

    def project(field):
        return lax.psum(jnp.sum(widened * field, axis=0), "mem")

    residual = smooth_rows(widened * (weight * extra[0])[None])
    total1 = project(smooth_rows(residual))
    image = residual + smooth_rows(widened * (weight * total1)[None])
    projected_image = project(smooth_rows(image))
    first_sums = all_sum(jnp.stack([squares(residual), weighted(total1)]))
    norm_now = first_sums[0]
    step1 = norm_now / (norm_now + first_sums[1])
    residual_next = residual - step1 * image
    norm_next = all_sum(jnp.stack([squares(residual_next)]))[0]
    beta = norm_next / norm_now
    direction = residual_next + beta * residual
    total2 = total1 - step1 * projected_image + beta * total1
    second_sums = all_sum(jnp.stack([squares(direction), weighted(total2)]))
    step2 = norm_next / (second_sums[0] + second_sums[1])
    increment = step1 * total1 + step2 * total2
    spread = lax.all_to_all(increment.reshape(grid_size, rows, nlon), "grid", 0, 0, tiled=True)
    whole = spread.reshape(levels, copies, rows, nlon)[:, 0]
    share = levels // mem_size
    mine_out = lax.dynamic_slice_in_dim(whole, mem_index * share, share, 0)
    recentred = (members.astype(jnp.float32) + whole[None]).astype(jnp.bfloat16)
    return (recentred, mine_out)


def solution(mesh):
    placed = (P("mem", None, "grid", None), P(None, "grid", None), P("grid", None), P())
    grid_size, mem_size = (mesh.shape["grid"], mesh.shape["mem"])
    body = local

    def chosen(members, innovation, observed_count, obs_precision):
        levels = members.shape[1]
        fits = (
            grid_size % levels == 0
            and grid_size // levels <= 2
            and (levels % mem_size == 0)
            and (ITERS == 2)
        )
        pick = local_by_level if fits else body
        return jax.shard_map(
            pick,
            mesh=mesh,
            in_specs=placed,
            out_specs=(P("mem", None, "grid", None), P("mem", "grid", None)),
            check_vma=False,
        )(members, innovation, observed_count, obs_precision)

    return chosen
```

profile of v0, /device:TPU:0, one launch (start us, length us, event | category | flops | bytes accessed | tf_op | source)
XLA Modules:
  0.0 122.1 jit_solution(157087438368064626)
XLA Ops:
  0.6 0.7 convert_bitcast_fusion.1
  1.4 0.7 fusion.63
  2.1 0.6 constant_dynamic-update-slice_fusion.7
  2.7 0.6 constant_dynamic-update-slice_fusion.6
  3.3 0.6 constant_dynamic-update-slice_fusion.5
  3.9 0.6 constant_dynamic-update-slice_fusion.4
  4.5 0.6 constant_dynamic-update-slice_fusion.3
  5.1 0.6 constant_dynamic-update-slice_fusion.2
  5.7 0.6 constant_dynamic-update-slice_fusion.1
  6.3 0.6 constant_dynamic-update-slice_fusion
  6.9 7.3 %all-to-all-start.1 = ((f32[8,2,2,512]{3,2,1,0:T(2,128)}), f32[8,2,2,512]{3,2,1,0:T(2,128)S(1)}, u32[]{:S(2)}, u32[]{:S(2)}) async-start(f32[8,2,2,512]{3,2,1,0:T(2,128)} %constant_dynamic-update-slice_fusion), calls=%async_computation.1 | async-start | bytes 131072 | tf_op jit(solution)/shard_map/all_to_all | solution.py:110
  14.2 0.6 bitcast_dynamic-update-slice_fusion.4
  14.9 0.6 bitcast_dynamic-update-slice_fusion.5
  15.5 0.6 bitcast_dynamic-update-slice_fusion.6
  16.1 0.6 bitcast_dynamic-update-slice_fusion.7
  16.8 0.6 bitcast_dynamic-update-slice_fusion.2
  17.4 0.6 bitcast_dynamic-update-slice_fusion.3
  18.1 0.6 bitcast_dynamic-update-slice_fusion
  18.7 0.6 bitcast_dynamic-update-slice_fusion.1
  19.3 1.8 %all-to-all-done.1 = f32[8,2,2,512]{3,2,1,0:T(2,128)S(1)} async-done(((f32[8,2,2,512]{3,2,1,0:T(2,128)}), f32[8,2,2,512]{3,2,1,0:T(2,128)S(1)}, u32[]{:S(2)}, u32[]{:S(2)}) %all-to-all-start.1) | async-done | bytes 65568 | tf_op jit(solution)/shard_map/all_to_all | solution.py:110
  21.1 4.2 %all-to-all-start = ((bf16[8,20,2,512]{3,2,1,0:T(2,128)(2,1)}), bf16[8,20,2,512]{3,2,1,0:T(2,128)(2,1)S(1)}, u32[]{:S(2)}, u32[]{:S(2)}) async-start(bf16[8,20,2,512]{3,2,1,0:T(2,128)(2,1)} %bitcast_dynamic-update-slice_fusion.1), calls=%async_computation | async-start | bytes 655360 | tf_op jit(solution)/shard_map/all_to_all | solution.py:104
  25.4 0.6 copy-done.1
  26.0 0.6 dynamic_slice.9
  26.7 0.7 fusion.61
  27.4 7.6 %all-to-all-done = bf16[8,20,2,512]{3,2,1,0:T(2,128)(2,1)S(1)} async-done(((bf16[8,20,2,512]{3,2,1,0:T(2,128)(2,1)}), bf16[8,20,2,512]{3,2,1,0:T(2,128)(2,1)S(1)}, u32[]{:S(2)}, u32[]{:S(2)}) %all-to-all-start) | async-done | bytes 327712 | tf_op jit(solution)/shard_map/all_to_all | solution.py:104
  35.3 0.4 copy.20
  35.7 0.5 reshape.161
  36.3 0.3 multiply_add_fusion.7
  36.7 0.3 multiply_add_fusion.6
  37.4 0.3 fusion.2
  38.1 0.9 select_reduce_fusion.2
  40.2 0.3 fusion.8
  40.9 0.4 fusion.13
  41.3 10.3 %psum.14 = f32[16,512]{1,0:T(8,128)S(1)} all-reduce(f32[16,512]{1,0:T(8,128)S(1)} %fusion.13), channel_id=1, replica_groups=mesh['grid'=8,'mem'=4] {'mem'}, use_global_device_ids=true, to_apply=%region_2.3 | all-reduce | flops 8192 | bytes 65536 | tf_op jit(solution)/shard_map/psum | solution.py:126
  51.6 0.7 select_reduce_fusion.3
  52.4 0.3 multiply_add_fusion.3
  53.1 0.8 fusion.46
  53.9 1.1 fusion.45
  55.5 0.7 select_maximum_fusion.1
  56.3 0.6 broadcast_in_dim.42
  56.9 3.8 %all-to-all-start.2 = ((f32[32,1,128]{2,1,0:T(1,128)}), f32[32,1,128]{2,1,0:T(1,128)S(1)}, u32[]{:S(2)}, u32[]{:S(2)}) async-start(f32[32,1,128]{2,1,0:T(1,128)} %broadcast_in_dim.42), calls=%async_computation.2 | async-start | bytes 32768 | tf_op jit(solution)/shard_map/all_to_all | solution.py:87
  60.7 1.5 %fusion.16 = f32[20,16,512]{2,1,0:T(8,128)S(1)} fusion(f32[20,16,512]{2,1,0:T(8,128)S(1)} %multiply_add_fusion.2, f32[20,16,511]{2,1,0:T(8,128)} %get-tuple-element.63, f32[20,16,1]{2,1,0:T(8,128)} %get-tuple-element.65, f32[20,16,1]{2,1,0:T(8,128)} %get-tuple-element.64, f32[20,16,511]{2,1,0:T(8,128)S(1)} %get-tuple-element.62), kind=kLoop, calls=%fused_computation.21 | loop fusion | flops 1146880 | bytes 2621440 | tf_op jit(solution)/shard_map/add | solution.py:80
  62.2 1.1 fusion.44
  63.3 0.8 fusion.43
  64.1 3.8 %all-to-all-done.2 = f32[32,1,128]{2,1,0:T(1,128)S(1)} async-done(((f32[32,1,128]{2,1,0:T(1,128)}), f32[32,1,128]{2,1,0:T(1,128)S(1)}, u32[]{:S(2)}, u32[]{:S(2)}) %all-to-all-start.2) | async-done | bytes 16416 | tf_op jit(solution)/shard_map/all_to_all | solution.py:87
  67.9 0.6 fusion.65
  70.2 2.1 %select_reduce_fusion.1 = (f32[]{:T(128)}, f32[20,16,512]{2,1,0:T(8,128)S(1)}) fusion(f32[20,16,512]{2,1,0:T(8,128)S(1)} %get-tuple-element.41, f32[]{:T(128)S(6)} %div.31, pred[16,512]{1,0:T(8,128)(4,1)S(1)} %select_compare_fusion, f32[20,16,512]{2,1,0:T(8,128)S(1)} %fusion.16, f32[20,16,1]{2,1,0:T(8,128)} %get-tuple-element.59, ...), kind=kLoop, calls=%fused_computation.41 | loop fusion | flops 2129919 | bytes 3285000 | tf_op jit(solution)/shard_map/reduce_sum | solution.py:120
  72.4 0.6 scatter.19
  73.0 0.6 broadcast_in_dim.43
  73.6 2.5 %all-to-all-start.3 = ((f32[32,1,128]{2,1,0:T(1,128)}), f32[32,1,128]{2,1,0:T(1,128)S(1)}, u32[]{:S(2)}, u32[]{:S(2)}) async-start(f32[32,1,128]{2,1,0:T(1,128)} %broadcast_in_dim.43), calls=%async_computation.3 | async-start | bytes 32768 | tf_op jit(solution)/shard_map/all_to_all | solution.py:87
  76.3 7.0 %all-to-all-done.3 = f32[32,1,128]{2,1,0:T(1,128)S(1)} async-done(((f32[32,1,128]{2,1,0:T(1,128)}), f32[32,1,128]{2,1,0:T(1,128)S(1)}, u32[]{:S(2)}, u32[]{:S(2)}) %all-to-all-start.3) | async-done | bytes 16416 | tf_op jit(solution)/shard_map/all_to_all | solution.py:87
  83.9 0.9 select_reduce_fusion
  85.6 0.3 fusion.23
  86.3 0.4 fusion.28
  86.7 10.4 %psum.15 = f32[16,512]{1,0:T(8,128)S(1)} all-reduce(f32[16,512]{1,0:T(8,128)S(1)} %fusion.28), channel_id=1, replica_groups=mesh['grid'=8,'mem'=4] {'mem'}, use_global_device_ids=true, to_apply=%region_9.10 | all-reduce | flops 8192 | bytes 65536 | tf_op jit(solution)/shard_map/psum | solution.py:126
  97.1 0.7 fusion.30
  98.4 0.7 select_maximum_fusion
  99.2 8.9 %all_to_all.33 = f32[32,1,128]{2,1,0:T(1,128)S(1)} all-to-all(f32[32,1,128]{2,1,0:T(1,128)S(1)} %broadcast_in_dim.44), channel_id=1, replica_groups=mesh['grid'=8,'mem'=4] {'grid','mem'}, dimensions={0} | all-to-all | bytes 32768 | tf_op jit(solution)/shard_map/all_to_all | solution.py:87
  108.2 0.6 fusion.64
  110.1 0.6 reshape.159
  110.7 3.3 %all-to-all-start.5 = ((f32[8,2,512]{2,1,0:T(2,128)}), f32[8,2,512]{2,1,0:T(2,128)S(1)}, u32[]{:S(2)}, u32[]{:S(2)}) async-start(f32[8,2,512]{2,1,0:T(2,128)} %reshape.159), calls=%async_computation.5 | async-start | bytes 65536 | tf_op jit(solution)/shard_map/all_to_all | solution.py:143
  114.1 6.6 %all-to-all-done.5 = f32[8,2,512]{2,1,0:T(2,128)S(1)} async-done(((f32[8,2,512]{2,1,0:T(2,128)}), f32[8,2,512]{2,1,0:T(2,128)S(1)}, u32[]{:S(2)}, u32[]{:S(2)}) %all-to-all-start.5) | async-done | bytes 32800 | tf_op jit(solution)/shard_map/all_to_all | solution.py:143
  120.7 0.8 add_convert_fusion
  121.5 0.6 dynamic-slice_bitcast_fusion
  (42 shorter events, 4.8 us)
Async XLA Ops:
  0.6 13.6 %copy-start = (bf16[20,4,2,512]{3,2,1,0:T(2,128)(2,1)S(1)}, bf16[20,4,2,512]{3,2,1,0:T(2,128)(2,1)}, u32[]{:S(2)}) copy-start(bf16[20,4,2,512]{3,2,1,0:T(2,128)(2,1)} %param.10) | copy-start | bytes 491524
  6.9 14.2 %all-to-all-start.1 = ((f32[8,2,2,512]{3,2,1,0:T(2,128)}), f32[8,2,2,512]{3,2,1,0:T(2,128)S(1)}, u32[]{:S(2)}, u32[]{:S(2)}) async-start(f32[8,2,2,512]{3,2,1,0:T(2,128)} %constant_dynamic-update-slice_fusion), calls=%async_computation.1 | async-start | bytes 131072 | tf_op jit(solution)/shard_map/all_to_all | solution.py:110
  21.1 13.9 %all-to-all-start = ((bf16[8,20,2,512]{3,2,1,0:T(2,128)(2,1)}), bf16[8,20,2,512]{3,2,1,0:T(2,128)(2,1)S(1)}, u32[]{:S(2)}, u32[]{:S(2)}) async-start(bf16[8,20,2,512]{3,2,1,0:T(2,128)(2,1)} %bitcast_dynamic-update-slice_fusion.1), calls=%async_computation | async-start | bytes 655360 | tf_op jit(solution)/shard_map/all_to_all | solution.py:104
  25.4 0.7 copy-start.1
  56.9 11.0 %all-to-all-start.2 = ((f32[32,1,128]{2,1,0:T(1,128)}), f32[32,1,128]{2,1,0:T(1,128)S(1)}, u32[]{:S(2)}, u32[]{:S(2)}) async-start(f32[32,1,128]{2,1,0:T(1,128)} %broadcast_in_dim.42), calls=%async_computation.2 | async-start | bytes 32768 | tf_op jit(solution)/shard_map/all_to_all | solution.py:87
  73.6 9.7 %all-to-all-start.3 = ((f32[32,1,128]{2,1,0:T(1,128)}), f32[32,1,128]{2,1,0:T(1,128)S(1)}, u32[]{:S(2)}, u32[]{:S(2)}) async-start(f32[32,1,128]{2,1,0:T(1,128)} %broadcast_in_dim.43), calls=%async_computation.3 | async-start | bytes 32768 | tf_op jit(solution)/shard_map/all_to_all | solution.py:87
  110.7 10.0 %all-to-all-start.5 = ((f32[8,2,512]{2,1,0:T(2,128)}), f32[8,2,512]{2,1,0:T(2,128)S(1)}, u32[]{:S(2)}, u32[]{:S(2)}) async-start(f32[8,2,512]{2,1,0:T(2,128)} %reshape.159), calls=%async_computation.5 | async-start | bytes 65536 | tf_op jit(solution)/shard_map/all_to_all | solution.py:143
where the time goes:
time: 123 us; the launch traced here: 122 us
  blocking collectives  29.6 us (24%)
  waiting for transfers between devices  26.8 us (22%)
  starting transfers between devices  21.2 us (17%)
  other arithmetic  19.5 us (16%)
  local copies, waits for them, and re-layouts  19.1 us (16%)
  between operations  5.99 us (5%)
    psum x2, blocking collectives, project(): return lax.psum(jnp.sum(widened * field, axis=0), 'mem')  20.7 us
    all_to_all x2, waiting for transfers between devices, all_sum(): lax.all_to_all(jnp.broadcast_to(row, (devices, 128)), ('grid', 'mem'), 0,...  10.7 us
    all_to_all x1, blocking collectives, all_sum(): lax.all_to_all(jnp.broadcast_to(row, (devices, 128)), ('grid', 'mem'), 0,...  8.95 us
    all_to_all x1, waiting for transfers between devices, local_by_level(): got = lax.all_to_all(sent, 'grid', 0, 0, tiled=True)  7.6 us
    all_to_all x1, starting transfers between devices, local_by_level(): extra = lax.all_to_all(extra, 'grid', 0, 0, tiled=True)  7.28 us
    all_to_all x1, waiting for transfers between devices, local_by_level(): lax.all_to_all(increment.reshape(grid_size, rows, nlon), 'grid', 0, 0, ti...  6.62 us
    all_to_all x2, starting transfers between devices, all_sum(): lax.all_to_all(jnp.broadcast_to(row, (devices, 128)), ('grid', 'mem'), 0,...  6.33 us
    unnamed x11, local copies, waits for them, and re-layouts  5.14 us
  transfers between devices with their start and end apart: 5, of which 5 were waited for; matrix products, arithmetic and copies ran while one was open for 8% of the time, Pallas kernels for 0%

commit v1 on v0

--- a/solution.py
+++ b/solution.py
@@ -123,7 +123,11 @@
         return jnp.where(first, jnp.sum(jnp.where(own, weight * total * total, 0.0)), 0.0)
 
     def project(field):
-        return lax.psum(jnp.sum(widened * field, axis=0), "mem")
+
+        def _compute_rails(slab_in):
+            return lax.all_gather(slab_in, axis_name="mem").sum(axis=0)
+
+        return _compute_rails(jnp.sum(widened * field, axis=0))
 
     residual = smooth_rows(widened * (weight * extra[0])[None])
     total1 = project(smooth_rows(residual))

time: 123 us -> 118 us (0.959)
  blocking collectives: 29.6 us -> 19.7 us
  other arithmetic: 19.5 us -> 21.5 us
  local copies, waits for them, and re-layouts: 19.1 us -> 20.4 us
    psum x2 -> x0, blocking collectives: 20.7 us -> none  [project(): return lax.psum(jnp.sum(widened * field, axis=0), 'mem')]
    all_gather x0 -> x2, blocking collectives: none -> 10.8 us  [_compute_rails(): return lax.all_gather(slab_in, axis_name='mem').sum(axis=0)]
    reduce_sum x3, other arithmetic: 0.06 us -> 2 us  [all_sum(): return jnp.sum(gathered, axis=0)]
    unnamed x11 -> x17, local copies, waits for them, and re-layouts: 5.14 us -> 6.46 us
  transfers between devices with their start and end apart: 5 -> 5, of which waited for: 5 -> 5; matrix products, arithmetic and copies ran while one was open for 8% -> 9% of each run, Pallas kernels for 0% -> 0%
where the time goes in v1:
time: 118 us; the launch traced here: 117 us
  waiting for transfers between devices  26.5 us (22%)
  starting transfers between devices  21.9 us (19%)
  other arithmetic  21.5 us (18%)
  local copies, waits for them, and re-layouts  20.4 us (17%)
  blocking collectives  19.7 us (17%)
  between operations  6.91 us (6%)
    all_gather x2, blocking collectives, _compute_rails(): return lax.all_gather(slab_in, axis_name='mem').sum(axis=0)  10.8 us
    all_to_all x2, waiting for transfers between devices, all_sum(): lax.all_to_all(jnp.broadcast_to(row, (devices, 128)), ('grid', 'mem'), 0,...  10.5 us
    all_to_all x1, blocking collectives, all_sum(): lax.all_to_all(jnp.broadcast_to(row, (devices, 128)), ('grid', 'mem'), 0,...  8.87 us
    all_to_all x1, waiting for transfers between devices, local_by_level(): got = lax.all_to_all(sent, 'grid', 0, 0, tiled=True)  7.6 us
    all_to_all x1, starting transfers between devices, local_by_level(): extra = lax.all_to_all(extra, 'grid', 0, 0, tiled=True)  7.28 us
    all_to_all x2, starting transfers between devices, all_sum(): lax.all_to_all(jnp.broadcast_to(row, (devices, 128)), ('grid', 'mem'), 0,...  7 us
    all_to_all x1, waiting for transfers between devices, local_by_level(): lax.all_to_all(increment.reshape(grid_size, rows, nlon), 'grid', 0, 0, ti...  6.62 us
    unnamed x17, local copies, waits for them, and re-layouts  6.46 us
  transfers between devices with their start and end apart: 5, of which 5 were waited for; matrix products, arithmetic and copies ran while one was open for 9% of the time, Pallas kernels for 0%

profile of v1, /device:TPU:0, one launch (start us, length us, event | category | flops | bytes accessed | tf_op | source)
XLA Modules:
  0.0 117.0 jit_solution(1675162444592671773)
XLA Ops:
  0.6 0.7 convert_bitcast_fusion.1
  1.4 0.7 fusion.68
  2.1 0.6 constant_dynamic-update-slice_fusion.7
  2.7 0.6 constant_dynamic-update-slice_fusion.6
  3.3 0.6 constant_dynamic-update-slice_fusion.5
  3.9 0.6 constant_dynamic-update-slice_fusion.4
  4.5 0.6 constant_dynamic-update-slice_fusion.3
  5.1 0.6 constant_dynamic-update-slice_fusion.2
  5.7 0.6 constant_dynamic-update-slice_fusion.1
  6.3 0.6 constant_dynamic-update-slice_fusion
  6.9 7.3 %all-to-all-start.1 = ((f32[8,2,2,512]{3,2,1,0:T(2,128)}), f32[8,2,2,512]{3,2,1,0:T(2,128)S(1)}, u32[]{:S(2)}, u32[]{:S(2)}) async-start(f32[8,2,2,512]{3,2,1,0:T(2,128)} %constant_dynamic-update-slice_fusion), calls=%async_computation.1 | async-start | bytes 131072 | tf_op jit(solution)/shard_map/all_to_all | solution.py:110
  14.2 0.6 bitcast_dynamic-update-slice_fusion.4
  14.9 0.6 bitcast_dynamic-update-slice_fusion.5
  15.5 0.7 bitcast_dynamic-update-slice_fusion.6
  16.2 0.6 bitcast_dynamic-update-slice_fusion.7
  16.8 0.6 bitcast_dynamic-update-slice_fusion.2
  17.4 0.6 bitcast_dynamic-update-slice_fusion.3
  18.1 0.6 bitcast_dynamic-update-slice_fusion
  18.7 0.6 bitcast_dynamic-update-slice_fusion.1
  19.4 1.7 %all-to-all-done.1 = f32[8,2,2,512]{3,2,1,0:T(2,128)S(1)} async-done(((f32[8,2,2,512]{3,2,1,0:T(2,128)}), f32[8,2,2,512]{3,2,1,0:T(2,128)S(1)}, u32[]{:S(2)}, u32[]{:S(2)}) %all-to-all-start.1) | async-done | bytes 65568 | tf_op jit(solution)/shard_map/all_to_all | solution.py:110
  21.1 4.3 %all-to-all-start = ((bf16[8,20,2,512]{3,2,1,0:T(2,128)(2,1)}), bf16[8,20,2,512]{3,2,1,0:T(2,128)(2,1)S(1)}, u32[]{:S(2)}, u32[]{:S(2)}) async-start(bf16[8,20,2,512]{3,2,1,0:T(2,128)(2,1)} %bitcast_dynamic-update-slice_fusion.1), calls=%async_computation | async-start | bytes 655360 | tf_op jit(solution)/shard_map/all_to_all | solution.py:104
  25.5 0.6 copy-done.4
  26.1 0.6 dynamic_slice.9
  26.8 0.7 fusion.66
  27.5 7.6 %all-to-all-done = bf16[8,20,2,512]{3,2,1,0:T(2,128)(2,1)S(1)} async-done(((bf16[8,20,2,512]{3,2,1,0:T(2,128)(2,1)}), bf16[8,20,2,512]{3,2,1,0:T(2,128)(2,1)S(1)}, u32[]{:S(2)}, u32[]{:S(2)}) %all-to-all-start) | async-done | bytes 327712 | tf_op jit(solution)/shard_map/all_to_all | solution.py:104
  35.4 0.4 copy.25
  35.7 0.5 reshape.280
  38.1 1.0 select_reduce_fusion.2
  40.3 0.3 fusion.8
  41.0 0.4 fusion.13
  41.4 5.4 %all-gather = f32[64,512]{1,0:T(8,128)S(1)} all-gather(f32[16,512]{1,0:T(8,128)S(1)} %fusion.13), channel_id=2, replica_groups=mesh['grid'=8,'mem'=4] {'mem'}, dimensions={0}, use_global_device_ids=true | all-gather | bytes 163840 | tf_op jit(solution)/shard_map/all_gather | solution.py:128
  47.8 0.8 fusion.51
  48.5 1.1 fusion.50
  49.6 0.7 fusion.32
  50.9 0.8 select_maximum_fusion.1
  51.7 0.6 broadcast_in_dim.42
  52.3 3.8 %all-to-all-start.2 = ((f32[32,1,128]{2,1,0:T(1,128)}), f32[32,1,128]{2,1,0:T(1,128)}, u32[]{:S(2)}, u32[]{:S(2)}) async-start(f32[32,1,128]{2,1,0:T(1,128)} %broadcast_in_dim.42), calls=%async_computation.2 | async-start | bytes 32768 | tf_op jit(solution)/shard_map/all_to_all | solution.py:87
  56.1 1.5 %fusion.16 = f32[20,16,512]{2,1,0:T(8,128)S(1)} fusion(f32[20,16,512]{2,1,0:T(8,128)S(1)} %multiply_add_fusion.2, f32[20,16,511]{2,1,0:T(8,128)} %get-tuple-element.61, f32[20,16,1]{2,1,0:T(8,128)} %get-tuple-element.63, f32[20,16,1]{2,1,0:T(8,128)} %get-tuple-element.62, f32[20,16,511]{2,1,0:T(8,128)S(1)} %get-tuple-element.60), kind=kLoop, calls=%fused_computation.21 | loop fusion | flops 1146880 | bytes 2621440 | tf_op jit(solution)/shard_map/add | solution.py:80
  57.6 1.1 fusion.49
  58.7 0.8 fusion.48
  59.5 3.6 %all-to-all-done.2 = f32[32,1,128]{2,1,0:T(1,128)} async-done(((f32[32,1,128]{2,1,0:T(1,128)}), f32[32,1,128]{2,1,0:T(1,128)}, u32[]{:S(2)}, u32[]{:S(2)}) %all-to-all-start.2) | async-done | bytes 16416 | tf_op jit(solution)/shard_map/all_to_all | solution.py:87
  63.1 0.7 reduce_sum.115
  63.8 0.6 fusion.70
  66.4 2.1 %select_reduce_fusion.1 = (f32[]{:T(128)}, f32[20,16,512]{2,1,0:T(8,128)S(1)}) fusion(f32[20,16,512]{2,1,0:T(8,128)S(1)} %get-tuple-element.41, f32[]{:T(128)S(6)} %div.37, pred[16,512]{1,0:T(8,128)(4,1)S(1)} %select_compare_fusion.1, f32[20,16,512]{2,1,0:T(8,128)S(1)} %fusion.16, f32[20,16,1]{2,1,0:T(8,128)} %get-tuple-element.57, ...), kind=kLoop, calls=%fused_computation.41 | loop fusion | flops 2129919 | bytes 3285000 | tf_op jit(solution)/shard_map/reduce_sum | solution.py:120
  68.5 0.6 scatter.19
  69.1 0.6 broadcast_in_dim.43
  69.7 3.2 %all-to-all-start.3 = ((f32[32,1,128]{2,1,0:T(1,128)}), f32[32,1,128]{2,1,0:T(1,128)}, u32[]{:S(2)}, u32[]{:S(2)}) async-start(f32[32,1,128]{2,1,0:T(1,128)} %broadcast_in_dim.43), calls=%async_computation.3 | async-start | bytes 32768 | tf_op jit(solution)/shard_map/all_to_all | solution.py:87
  73.0 6.9 %all-to-all-done.3 = f32[32,1,128]{2,1,0:T(1,128)} async-done(((f32[32,1,128]{2,1,0:T(1,128)}), f32[32,1,128]{2,1,0:T(1,128)}, u32[]{:S(2)}, u32[]{:S(2)}) %all-to-all-start.3) | async-done | bytes 16416 | tf_op jit(solution)/shard_map/all_to_all | solution.py:87
  80.0 1.2 %reduce_sum.117 = f32[128]{0:T(128)} reduce(f32[32,1,128]{2,0,1:T(8,128)} %bitcast.20, f32[]{:T(128)} %constant.131.clone.1), dimensions={0,1}, to_apply=%region_6.7 | reduce | flops 3968 | bytes 16900 | tf_op jit(solution)/shard_map/reduce_sum | solution.py:90
  82.6 0.9 select_reduce_fusion
  84.3 0.3 fusion.23
  85.0 0.4 fusion.28
  85.4 5.4 %all-gather.1 = f32[64,512]{1,0:T(8,128)S(1)} all-gather(f32[16,512]{1,0:T(8,128)S(1)} %fusion.28), channel_id=3, replica_groups=mesh['grid'=8,'mem'=4] {'mem'}, dimensions={0}, use_global_device_ids=true | all-gather | bytes 163840 | tf_op jit(solution)/shard_map/all_gather | solution.py:128
  90.9 0.6 copy-done.2
  91.5 0.7 fusion.33
  92.9 0.6 select_maximum_fusion
  93.5 8.9 %all_to_all.33 = f32[32,1,128]{2,1,0:T(1,128)S(1)} all-to-all(f32[32,1,128]{2,1,0:T(1,128)S(1)} %broadcast_in_dim.44), channel_id=1, replica_groups=mesh['grid'=8,'mem'=4] {'grid','mem'}, dimensions={0} | all-to-all | bytes 32768 | tf_op jit(solution)/shard_map/all_to_all | solution.py:87
  102.4 0.6 fusion.69
  104.2 0.6 copy-done.3
  104.9 0.6 reshape.281
  105.6 3.3 %all-to-all-start.5 = ((f32[8,2,512]{2,1,0:T(2,128)}), f32[8,2,512]{2,1,0:T(2,128)S(1)}, u32[]{:S(2)}, u32[]{:S(2)}) async-start(f32[8,2,512]{2,1,0:T(2,128)} %reshape.281), calls=%async_computation.5 | async-start | bytes 65536 | tf_op jit(solution)/shard_map/all_to_all | solution.py:147
  108.9 6.6 %all-to-all-done.5 = f32[8,2,512]{2,1,0:T(2,128)S(1)} async-done(((f32[8,2,512]{2,1,0:T(2,128)}), f32[8,2,512]{2,1,0:T(2,128)S(1)}, u32[]{:S(2)}, u32[]{:S(2)}) %all-to-all-start.5) | async-done | bytes 32800 | tf_op jit(solution)/shard_map/all_to_all | solution.py:147
  115.6 0.8 add_convert_fusion
  116.4 0.6 dynamic-slice_bitcast_fusion
  (56 shorter events, 5.9 us)
Async XLA Ops:
  0.6 13.6 %copy-start = (bf16[20,4,2,512]{3,2,1,0:T(2,128)(2,1)S(1)}, bf16[20,4,2,512]{3,2,1,0:T(2,128)(2,1)}, u32[]{:S(2)}) copy-start(bf16[20,4,2,512]{3,2,1,0:T(2,128)(2,1)} %param.10) | copy-start | bytes 491524
  6.9 14.2 %all-to-all-start.1 = ((f32[8,2,2,512]{3,2,1,0:T(2,128)}), f32[8,2,2,512]{3,2,1,0:T(2,128)S(1)}, u32[]{:S(2)}, u32[]{:S(2)}) async-start(f32[8,2,2,512]{3,2,1,0:T(2,128)} %constant_dynamic-update-slice_fusion), calls=%async_computation.1 | async-start | bytes 131072 | tf_op jit(solution)/shard_map/all_to_all | solution.py:110
  19.4 30.2 %copy-start.1 = (pred[8,2]{1,0:T(8,128)(4,1)}, pred[8,2]{1,0:T(8,128)(4,1)S(1)}, u32[]{:S(2)}) copy-start(pred[8,2]{1,0:T(8,128)(4,1)S(1)} %fusion.39) | copy-start | bytes 52
  21.1 14.0 %all-to-all-start = ((bf16[8,20,2,512]{3,2,1,0:T(2,128)(2,1)}), bf16[8,20,2,512]{3,2,1,0:T(2,128)(2,1)S(1)}, u32[]{:S(2)}, u32[]{:S(2)}) async-start(bf16[8,20,2,512]{3,2,1,0:T(2,128)(2,1)} %bitcast_dynamic-update-slice_fusion.1), calls=%async_computation | async-start | bytes 655360 | tf_op jit(solution)/shard_map/all_to_all | solution.py:104
  25.4 0.7 copy-start.4
  52.3 10.8 %all-to-all-start.2 = ((f32[32,1,128]{2,1,0:T(1,128)}), f32[32,1,128]{2,1,0:T(1,128)}, u32[]{:S(2)}, u32[]{:S(2)}) async-start(f32[32,1,128]{2,1,0:T(1,128)} %broadcast_in_dim.42), calls=%async_computation.2 | async-start | bytes 32768 | tf_op jit(solution)/shard_map/all_to_all | solution.py:87
  69.7 10.3 %all-to-all-start.3 = ((f32[32,1,128]{2,1,0:T(1,128)}), f32[32,1,128]{2,1,0:T(1,128)}, u32[]{:S(2)}, u32[]{:S(2)}) async-start(f32[32,1,128]{2,1,0:T(1,128)} %broadcast_in_dim.43), calls=%async_computation.3 | async-start | bytes 32768 | tf_op jit(solution)/shard_map/all_to_all | solution.py:87
  90.8 0.7 copy-start.2
  104.2 0.7 copy-start.3
  105.6 10.0 %all-to-all-start.5 = ((f32[8,2,512]{2,1,0:T(2,128)}), f32[8,2,512]{2,1,0:T(2,128)S(1)}, u32[]{:S(2)}, u32[]{:S(2)}) async-start(f32[8,2,512]{2,1,0:T(2,128)} %reshape.281), calls=%async_computation.5 | async-start | bytes 65536 | tf_op jit(solution)/shard_map/all_to_all | solution.py:147
